TPU v7x, 256 devices: a whole 4x4x8 slice. The times are simulated.
256 devices in a mesh: grp: 4 (over y), ex: 8 (over x, core), tp: 8 (over z).
Axes of the slice: x: 4, y: 4, z: 8, core: 2. Of those that a mesh axis runs over, the one named last changes fastest.
Arguments:
- residual: bfloat16 [512, 2, 6144], P(('grp', 'ex'), None, 'tp'), may hold values from -34 to 34
- query_new: bfloat16 [512, 2, 6144], P(('grp', 'ex'), None, 'tp'), may hold values from -5 to 5
- key_new: bfloat16 [512, 2, 1024], P(('grp', 'ex'), None, 'tp'), may hold values from -8 to 8
- value_new: bfloat16 [512, 2, 1024], P(('grp', 'ex'), None, 'tp'), may hold values from -12 to 12
- key_cache: bfloat16 [512, 8, 512, 128], P(('grp', 'ex'), 'tp'), may hold values from -5 to 5
- value_cache: bfloat16 [512, 8, 512, 128], P(('grp', 'ex'), 'tp'), may hold values from -12 to 12
- lengths: int32 [512], P(('grp', 'ex')), may hold values from 128 to 512, as said below
- norm_gain: bfloat16 [6144], P('tp'), may hold values from 0.099609375 to 1.8984375
- router: float32 [6144, 8], P('tp'), may hold values from -0.078125 to 0.078125
- routes: int32 [512, 2, 2], P(('grp', 'ex')), may hold values from 0 to 7, all different within a row; in each aligned block of 32 rows (0 to 31, 32 to 63, ..., all dimensions but the last counted through in order) at most 16 rows name the same one
- w_gate: bfloat16 [8, 6144, 8192], P('ex', None, ('grp', 'tp')), may hold values from -0.078125 to 0.078125
- w_up: bfloat16 [8, 6144, 8192], P('ex', None, ('grp', 'tp')), may hold values from -0.078125 to 0.078125
- w_down: bfloat16 [8, 8192, 6144], P('ex', ('grp', 'tp')), may hold values from -0.125 to 0.125
Outputs:
- attended: bfloat16 [512, 2, 6144], P(('grp', 'ex'), None, 'tp')
- expert_mix: bfloat16 [512, 2, 6144], P(('grp', 'ex'), None, 'tp')
Inputs may be any that keep to these rules, and one draw needn't show every extreme that they name: `routes`: over the rows of one device (aligned blocks of 32 rows, environments then steps) no expert is named more than 16 times, and in some blocks one is named exactly 16 times; a row's two experts differ. `lengths`: some environment's cache is full.
All inputs are finite; a program needn't handle non-finite values.
Results may differ from a plain program's by a relative error of at most 0.023.
Values may be sent and summed in bfloat16 or wider, within the bound.
No kernel may reach another device: no remote copies, remote signals or barrier semaphores. Data moves between devices by JAX's collectives and lax.ppermute only.
A program may use at most 128 MiB of HBM per device.

v0:
```python
import jax
import jax.numpy as jnp
from jax import lax
from jax.sharding import PartitionSpec as P

CAP = 16


def attend(query_new, key_new, value_new, key_cache, value_cache, lengths):
    env_count, step_count, feature_count = query_new.shape
    kv_count = key_cache.shape[1]
    context = key_cache.shape[2]
    head_dim = key_cache.shape[3]
    group_size = feature_count // (kv_count * head_dim)
    queries = query_new.reshape(env_count, step_count, kv_count, group_size, head_dim)
    keys_now = key_new.reshape(env_count, step_count, kv_count, head_dim)
    values_now = value_new.reshape(env_count, step_count, kv_count, head_dim)
    score_scale = head_dim ** (-0.5)
    cached = (
        jnp.einsum("eskgd,ekcd->eskgc", queries, key_cache, preferred_element_type=jnp.float32)
        * score_scale
    )
    fresh_scores = (
        jnp.einsum("eskgd,etkd->eskgt", queries, keys_now, preferred_element_type=jnp.float32)
        * score_scale
    )
    valid_mask = (lax.broadcasted_iota(jnp.int32, (env_count, context), 1) < lengths[:, None])[
        :, None, None, None, :
    ]
    causal = (
        lax.broadcasted_iota(jnp.int32, (step_count, step_count), 1)
        <= lax.broadcasted_iota(jnp.int32, (step_count, step_count), 0)
    )[None, :, None, None, :]
    cached = jnp.where(valid_mask, cached, -1e30)
    fresh_scores = jnp.where(causal, fresh_scores, -1e30)
    row_top = jnp.maximum(jnp.max(cached, -1), jnp.max(fresh_scores, -1))[..., None]
    weight_cached = jnp.where(valid_mask, jnp.exp(cached - row_top), 0.0)
    weight_fresh = jnp.where(causal, jnp.exp(fresh_scores - row_top), 0.0)
    row_total = (jnp.sum(weight_cached, -1) + jnp.sum(weight_fresh, -1))[..., None]
    probs_cached = (weight_cached / row_total).astype(jnp.bfloat16)
    probs_fresh = (weight_fresh / row_total).astype(jnp.bfloat16)
    heads_out = jnp.einsum(
        "eskgc,ekcd->eskgd", probs_cached, value_cache, preferred_element_type=jnp.float32
    )
    heads_out = heads_out + jnp.einsum(
        "eskgt,etkd->eskgd", probs_fresh, values_now, preferred_element_type=jnp.float32
    )
    return heads_out.reshape(env_count, step_count, feature_count)


def per_device(
    residual,
    query_new,
    key_new,
    value_new,
    key_cache,
    value_cache,
    lengths,
    norm_gain,
    router,
    routes,
    w_gate,
    w_up,
    w_down,
):
    env_count, step_count, slice_width = residual.shape
    local_experts, width, hidden_local = w_gate.shape
    experts = router.shape[1]
    topk = routes.shape[2]
    group_count = lax.axis_size("grp")
    tensor_count = lax.axis_size("tp")
    owner_count = lax.axis_size("ex")
    row_count = env_count * step_count
    state = residual.astype(jnp.float32) + attend(
        query_new, key_new, value_new, key_cache, value_cache, lengths
    )
    attended = state.astype(jnp.bfloat16)
    squares = jnp.sum(state * state, -1)
    scaled = state * norm_gain.astype(jnp.float32)
    partial_logits = jnp.einsum("esd,dx->esx", scaled, router, precision=lax.Precision.HIGHEST)
    squares, logits = lax.psum((squares, partial_logits), "tp")
    root_mean = jnp.sqrt(squares / width + 1e-05)[..., None]
    logits = logits / root_mean
    normed = (scaled / root_mean).astype(jnp.bfloat16)
    expert_ids = lax.broadcasted_iota(jnp.int32, (1, 1, 1, experts), 3)
    picked_logits = jnp.sum(
        jnp.where(routes[..., None] == expert_ids, logits[:, :, None, :], 0.0), -1
    )
    first_gate = 1.0 / (1.0 + jnp.exp(picked_logits[..., 1] - picked_logits[..., 0]))
    second_gate = 1.0 - first_gate
    flat_routes = routes.reshape(row_count * topk)
    expert_hits = (flat_routes[:, None] == lax.broadcasted_iota(jnp.int32, (1, experts), 1)).astype(
        jnp.int32
    )
    earlier = jnp.cumsum(expert_hits, axis=0) - expert_hits
    slot_ids = jnp.sum(earlier * expert_hits, axis=1)
    targets = flat_routes * CAP + slot_ids
    slot_table = lax.broadcasted_iota(jnp.int32, (1, experts * CAP), 1)
    placed = (
        (targets[:, None] == slot_table)
        .astype(jnp.bfloat16)
        .reshape(row_count, topk, experts * CAP)
    )
    sender = jnp.sum(placed, axis=1)
    packed = jnp.einsum(
        "rs,rd->sd",
        sender,
        normed.reshape(row_count, slice_width),
        preferred_element_type=jnp.float32,
    )
    outgoing = packed.astype(jnp.bfloat16).reshape(experts, CAP, slice_width)
    received = lax.all_to_all(outgoing, "ex", split_axis=0, concat_axis=0, tiled=True)
    received = received.reshape(1, owner_count, local_experts, CAP, slice_width)
    pieces = lax.all_gather(received, ("grp", "tp"), axis=0, tiled=True)
    pieces = pieces.reshape(group_count, tensor_count, owner_count, local_experts, CAP, slice_width)
    gate_split = w_gate.reshape(local_experts, tensor_count, slice_width, hidden_local)
    up_split = w_up.reshape(local_experts, tensor_count, slice_width, hidden_local)
    gate_sums = jnp.einsum(
        "gtajcd,jtdf->jgacf", pieces, gate_split, preferred_element_type=jnp.float32
    )
    up_sums = jnp.einsum("gtajcd,jtdf->jgacf", pieces, up_split, preferred_element_type=jnp.float32)
    hidden = (jax.nn.silu(gate_sums) * up_sums).astype(jnp.bfloat16)
    down_split = w_down.reshape(local_experts, hidden_local, tensor_count, slice_width)
    down_terms = jnp.einsum(
        "jgacf,jftd->gtajcd", hidden, down_split, preferred_element_type=jnp.float32
    )
    down_terms = down_terms.reshape(
        group_count * tensor_count, owner_count, local_experts, CAP, slice_width
    )
    summed = lax.psum_scatter(
        down_terms.astype(jnp.bfloat16), ("grp", "tp"), scatter_dimension=0, tiled=True
    ).astype(jnp.float32)
    returned = lax.all_to_all(
        summed[0].astype(jnp.bfloat16), "ex", split_axis=0, concat_axis=0, tiled=True
    )
    returned = returned.reshape(experts * CAP, slice_width)
    picked_rows = jnp.einsum("rks,sd->rkd", placed, returned, preferred_element_type=jnp.float32)
    picked_rows = picked_rows.reshape(env_count, step_count, topk, slice_width)
    expert_mix = (
        first_gate[..., None] * picked_rows[:, :, 0] + second_gate[..., None] * picked_rows[:, :, 1]
    )
    return (attended, expert_mix.astype(jnp.bfloat16))


def solution(mesh):
    return jax.shard_map(
        per_device,
        mesh=mesh,
        in_specs=(
            P(("grp", "ex"), None, "tp"),
            P(("grp", "ex"), None, "tp"),
            P(("grp", "ex"), None, "tp"),
            P(("grp", "ex"), None, "tp"),
            P(("grp", "ex"), "tp", None, None),
            P(("grp", "ex"), "tp", None, None),
            P(("grp", "ex")),
            P("tp"),
            P("tp", None),
            P(("grp", "ex"), None, None),
            P("ex", None, ("grp", "tp")),
            P("ex", None, ("grp", "tp")),
            P("ex", ("grp", "tp"), None),
        ),
        out_specs=(P(("grp", "ex"), None, "tp"), P(("grp", "ex"), None, "tp")),
        check_vma=False,
    )
```

profile of v0, /device:TPU:1, one launch (start us, length us, event | category | flops | bytes accessed | tf_op | source)
XLA Modules:
  0.0 389.3 jit_solution(13137319937710696107)
XLA Ops:
  7.2 0.0 copy-start
  7.2 0.0 all-gather.3.cloned.1.call-start
  7.2 0.8 broadcast_multiply_fusion
  8.1 0.8 copy.92
  8.9 0.8 reshape.262
  9.8 0.9 iota_compare_fusion.3
  10.6 2.3 fusion.55
  13.0 1.1 fusion.56
  14.2 0.3 fusion.28
  14.5 0.1 fusion.50
  14.6 0.3 fusion.46
  14.9 0.5 fusion.23
  15.4 0.1 reshape.261
  15.5 0.1 multiply_reduce_fusion
  15.6 0.5 fusion.37
  16.1 17.7 %all-reduce = (f32[16,2]{0,1:T(2,128)S(1)}, f32[16,2,8]{0,2,1:T(8,128)S(1)}) all-reduce(f32[16,2]{0,1:T(2,128)S(1)} %multiply_reduce_fusion, f32[16,2,8]{0,2,1:T(8,128)S(1)} %fusion.37), channel_id=1, replica_groups=mesh['grp'=4,'ex'=8,'tp'=8] {'tp'}, use_global_device_ids=true, to_apply=%region_6.7 | all-reduce | flops 288 | bytes 2304 | tf_op jit(solution)/shard_map/psum | solution.py:81
  33.8 0.1 divide_convert_fusion.2
  33.9 0.1 copy.91
  34.0 0.1 mul.92
  34.1 0.1 eq.68
  34.2 0.1 fusion.40
  34.3 0.1 reduce_window_sum.11
  34.4 0.2 select_reduce_fusion
  34.6 0.1 reduce_sum.64
  34.7 0.1 copy.93
  34.8 0.1 fusion.45
  34.8 0.1 copy.94
  34.9 0.2 convolution_convert_fusion
  35.2 14.4 %all_to_all.10 = bf16[8,16,768]{2,1,0:T(8,128)(2,1)} all-to-all(bf16[8,16,768]{2,1,0:T(8,128)(2,1)S(1)} %bitcast.164), channel_id=1, replica_groups=mesh['grp'=4,'ex'=8,'tp'=8] {'ex'}, dimensions={0} | all-to-all | bytes 393216 | tf_op jit(solution)/shard_map/all_to_all | solution.py:112
  49.5 0.0 all-gather.3.cloned.1.call-update
  49.5 0.0 reduce-scatter.2.cloned.1.call-start
  49.6 4.5 %copy.120 = bf16[32,8,8,768]{3,2,1,0:T(8,128)(2,1)} copy(bf16[32,8,8,768]{3,1,2,0:T(8,128)(2,1)} %bitcast.162) | data formatting | bytes 6291456
  54.1 79.5 %all-gather.3.cloned.1.call-done = bf16[256,16,768]{2,1,0:T(8,128)(2,1)} async-done(((bf16[8,16,768]{2,1,0:T(8,128)(2,1)}), bf16[256,16,768]{2,1,0:T(8,128)(2,1)}) %all-gather.3.cloned.1.call-update) | async-done | bytes 6291472 | tf_op jit(solution)/shard_map/all_gather | solution.py:114
  133.6 4.7 %convolution_bitcast_fusion.1 = f32[4,8,16,256]{3,2,1,0:T(8,128)S(1)} fusion(bf16[4,8,8,16,768]{4,3,2,1,0:T(8,128)(2,1)} %bitcast.168, bf16[8,768,256,1,1]{2,1,4,0,3:T(8,128)(2,1)S(1)} %bitcast.159), kind=kOutput, calls=%fused_computation.8 | convolution fusion | flops 1610612736 | bytes 9961472 | tf_op jit(solution)/shard_map/gtajcd,jtdf->jgacf/dot_general | solution.py:118
  138.3 0.8 copy-done.7
  139.1 1.8 fusion.19
  140.9 0.1 copy-done.1
  141.0 1.9 convert_bitcast_fusion
  142.9 3.5 copy.98
  146.5 0.0 reduce-scatter.2.cloned.1.call-update
  146.5 0.7 copy.102
  147.2 0.1 iota_compare_fusion.1
  147.3 219.0 %reduce-scatter.2.cloned.1.call-done = bf16[1,8,1,16,768]{4,3,1,0,2:T(8,128)(2,1)} async-done(((bf16[32,8,1,16,768]{4,3,1,0,2:T(8,128)(2,1)}), bf16[1,8,1,16,768]{4,3,1,0,2:T(8,128)(2,1)}) %reduce-scatter.2.cloned.1.call-update) | async-done | bytes 196624 | tf_op jit(solution)/shard_map/reduce_scatter | solution.py:130
  366.3 9.4 %all-to-all-start.1 = ((bf16[8,1,16,768]{3,2,1,0:T(8,128)(2,1)}), bf16[8,1,16,768]{3,2,1,0:T(8,128)(2,1)S(1)}, u32[]{:S(2)}, u32[]{:S(2)}) async-start(bf16[8,1,16,768]{3,2,1,0:T(8,128)(2,1)} %bitcast.165), calls=%async_computation.2 | async-start | bytes 393216 | tf_op jit(solution)/shard_map/all_to_all | solution.py:133
  375.7 5.8 %all-to-all-done.1 = bf16[8,1,16,768]{3,2,1,0:T(8,128)(2,1)S(1)} async-done(((bf16[8,1,16,768]{3,2,1,0:T(8,128)(2,1)}), bf16[8,1,16,768]{3,2,1,0:T(8,128)(2,1)S(1)}, u32[]{:S(2)}, u32[]{:S(2)}) %all-to-all-start.1) | async-done | bytes 196640 | tf_op jit(solution)/shard_map/all_to_all | solution.py:133
  381.6 0.2 fusion.42
  381.7 0.1 fusion.35
  381.8 0.7 copy.103
  (28 shorter events, 0.2 us)
Async XLA Ops:
  7.2 126.4 %copy-start = (bf16[1,6144,256]{2,1,0:T(8,128)(2,1)S(1)}, bf16[1,6144,256]{2,1,0:T(8,128)(2,1)}, u32[]{:S(2)}) copy-start(bf16[1,6144,256]{2,1,0:T(8,128)(2,1)} %param.23) | copy-start | bytes 9437188
  7.2 7.4 %copy-start.9 = (bf16[16,2,128]{2,1,0:T(2,128)(2,1)S(1)}, bf16[16,2,128]{2,1,0:T(2,128)(2,1)}, u32[]{:S(2)}) copy-start(bf16[16,2,128]{2,1,0:T(2,128)(2,1)} %param.16) | copy-start | bytes 24580
  7.2 126.4 %all-gather.3.cloned.1.call-start = ((), (), s32[]{:S(2)}) async-start(), calls=%async_computation.4 | async-start | bytes 6488064 | tf_op jit(solution)/shard_map/all_gather | solution.py:114
  9.8 5.2 %copy-start.8 = (bf16[16,1,512,128]{3,2,1,0:T(8,128)(2,1)S(1)}, bf16[16,1,512,128]{3,2,1,0:T(8,128)(2,1)}, u32[]{:S(2)}) copy-start(bf16[16,1,512,128]{3,2,1,0:T(8,128)(2,1)} %param.18) | copy-start | bytes 6291460
  13.0 2.5 copy-start.5
  13.0 2.5 copy-start.2
  13.0 2.6 copy-start.3
  49.5 316.7 %reduce-scatter.2.cloned.1.call-start = ((), (), s32[]{:S(2)}) async-start(), calls=%async_computation.3 | async-start | bytes 6488064 | tf_op jit(solution)/shard_map/reduce_scatter | solution.py:130
  133.6 4.7 %copy-start.6 = (bf16[256,16,768]{2,1,0:T(8,128)(2,1)S(1)}, bf16[256,16,768]{2,1,0:T(8,128)(2,1)}, u32[]{:S(2)}) copy-start(bf16[256,16,768]{2,1,0:T(8,128)(2,1)} %all-gather.3.cloned.1.call-done) | copy-start | bytes 18874372
  133.6 5.5 %copy-start.7 = (bf16[1,6144,256]{2,1,0:T(8,128)(2,1)S(1)}, bf16[1,6144,256]{2,1,0:T(8,128)(2,1)}, u32[]{:S(2)}) copy-start(bf16[1,6144,256]{2,1,0:T(8,128)(2,1)} %param.24) | copy-start | bytes 9437188
  139.1 1.9 copy-start.1
  146.5 0.8 copy-start.4
  366.3 15.3 %all-to-all-start.1 = ((bf16[8,1,16,768]{3,2,1,0:T(8,128)(2,1)}), bf16[8,1,16,768]{3,2,1,0:T(8,128)(2,1)S(1)}, u32[]{:S(2)}, u32[]{:S(2)}) async-start(bf16[8,1,16,768]{3,2,1,0:T(8,128)(2,1)} %bitcast.165), calls=%async_computation.2 | async-start | bytes 393216 | tf_op jit(solution)/shard_map/all_to_all | solution.py:133
Sparse Core Ops, SparseCore 0:
  49.7 83.8 all-gather.2
  146.6 219.6 reduce-scatter.1
where the time goes:
time: 390 us; the launch traced here: 389 us
  waiting for transfers between devices  304 us (78%)
  blocking collectives  32 us (8%)
  between operations  14.3 us (4%)
  matrix products  13.5 us (3%)
  local copies, waits for them, and re-layouts  12.6 us (3%)
  starting transfers between devices  9.5 us (2%)
    reduce_scatter x1, waiting for transfers between devices, per_device(): lax.psum_scatter(down_terms.astype(jnp.bfloat16), ('grp', 'tp'), scatter_...  219 us
    all_gather x1, waiting for transfers between devices, per_device(): pieces = lax.all_gather(received, ('grp', 'tp'), axis=0, tiled=True)  79.5 us
    psum x1, blocking collectives, per_device(): squares, logits = lax.psum((squares, partial_logits), 'tp')  17.7 us
    all_to_all x1, blocking collectives, per_device(): lax.all_to_all(outgoing, 'ex', split_axis=0, concat_axis=0, tiled=True)  14.4 us
    all_to_all x1, starting transfers between devices, per_device(): lax.all_to_all(summed[0].astype(jnp.bfloat16), 'ex', split_axis=0, concat...  9.42 us
  transfers between devices with their start and end apart: 3, of which 3 were waited for; matrix products, arithmetic and copies ran while one was open for 1% of the time, Pallas kernels for 0%

commit v1 on v0

--- a/solution.py
+++ b/solution.py
@@ -1,9 +1,26 @@
+import functools
 import jax
 import jax.numpy as jnp
 from jax import lax
 from jax.sharding import PartitionSpec as P
 
 CAP = 16
+
+
+def draw_the_packet(view, which_axis):
+    carry_out = jnp.concatenate(
+        lax.all_to_all(
+            jnp.stack([view] * lax.axis_size(which_axis), 0),
+            axis_name=which_axis,
+            split_axis=0,
+            concat_axis=0,
+        ),
+        0,
+    )
+    return carry_out
+
+
+finish_tracks = functools.partial(draw_the_packet, which_axis=("grp", "tp"))
 
 
 def attend(query_new, key_new, value_new, key_cache, value_cache, lengths):
@@ -111,7 +128,7 @@
     outgoing = packed.astype(jnp.bfloat16).reshape(experts, CAP, slice_width)
     received = lax.all_to_all(outgoing, "ex", split_axis=0, concat_axis=0, tiled=True)
     received = received.reshape(1, owner_count, local_experts, CAP, slice_width)
-    pieces = lax.all_gather(received, ("grp", "tp"), axis=0, tiled=True)
+    pieces = finish_tracks(received)
     pieces = pieces.reshape(group_count, tensor_count, owner_count, local_experts, CAP, slice_width)
     gate_split = w_gate.reshape(local_experts, tensor_count, slice_width, hidden_local)
     up_split = w_up.reshape(local_experts, tensor_count, slice_width, hidden_local)

time: 390 us -> 457 us (1.17)
  waiting for transfers between devices: 304 us -> 360 us
  starting transfers between devices: 9.5 us -> 15.9 us
    all_to_all x0 -> x1, waiting for transfers between devices: none -> 136 us  [draw_the_packet(): lax.all_to_all(jnp.stack([view] * lax.axis_size(which_axis), 0), axis_nam...]
    all_gather x1 -> x0, waiting for transfers between devices: 79.5 us -> none  [per_device(): pieces = lax.all_gather(received, ('grp', 'tp'), axis=0, tiled=True)]
    all_to_all x0 -> x1, starting transfers between devices: none -> 6.49 us  [draw_the_packet(): lax.all_to_all(jnp.stack([view] * lax.axis_size(which_axis), 0), axis_nam...]
where the time goes in v1:
time: 457 us
  waiting for transfers between devices  360 us (79%)
  blocking collectives  31.9 us (7%)
  matrix products  16.5 us (4%)
  starting transfers between devices  15.9 us (3%)
  local copies, waits for them, and re-layouts  15.1 us (3%)
  between operations  14.3 us (3%)
    reduce_scatter x1, waiting for transfers between devices, per_device(): lax.psum_scatter(down_terms.astype(jnp.bfloat16), ('grp', 'tp'), scatter_...  218 us
    all_to_all x1, waiting for transfers between devices, draw_the_packet(): lax.all_to_all(jnp.stack([view] * lax.axis_size(which_axis), 0), axis_nam...  136 us
    psum x1, blocking collectives, per_device(): squares, logits = lax.psum((squares, partial_logits), 'tp')  17.7 us
    all_to_all x1, blocking collectives, per_device(): lax.all_to_all(outgoing, 'ex', split_axis=0, concat_axis=0, tiled=True)  14.2 us
    all_to_all x1, starting transfers between devices, per_device(): lax.all_to_all(summed[0].astype(jnp.bfloat16), 'ex', split_axis=0, concat...  9.39 us
  transfers between devices with their start and end apart: 3, of which 3 were waited for; matrix products, arithmetic and copies ran while one was open for 1% of the time, Pallas kernels for 0%

profile of v1, /device:TPU:1, one launch (start us, length us, event | category | flops | bytes accessed | tf_op | source)
XLA Modules:
  0.0 456.8 jit_solution(5945550306415619645)
XLA Ops:
  7.2 0.0 copy-start
  7.2 0.8 broadcast_multiply_fusion
  8.0 0.9 copy.92
  8.9 0.8 reshape.257
  9.8 0.0 copy-start.7
  9.8 0.9 iota_compare_fusion.3
  10.6 2.3 fusion.55
  13.0 0.0 copy-start.2
  13.0 1.1 fusion.56
  14.2 0.3 fusion.28
  14.5 0.1 fusion.50
  14.6 0.3 fusion.46
  14.9 0.5 fusion.23
  15.5 0.1 reshape.256
  15.6 0.1 multiply_reduce_fusion
  15.7 0.5 fusion.37
  16.1 17.7 %all-reduce = (f32[16,2]{0,1:T(2,128)S(1)}, f32[16,2,8]{0,2,1:T(8,128)S(1)}) all-reduce(f32[16,2]{0,1:T(2,128)S(1)} %multiply_reduce_fusion, f32[16,2,8]{0,2,1:T(8,128)S(1)} %fusion.37), channel_id=1, replica_groups=mesh['grp'=4,'ex'=8,'tp'=8] {'tp'}, use_global_device_ids=true, to_apply=%region_6.7 | all-reduce | flops 288 | bytes 2304 | tf_op jit(solution)/shard_map/psum | solution.py:98
  33.8 0.1 divide_convert_fusion.2
  33.9 0.1 copy.91
  34.0 0.1 mul.92
  34.1 0.1 eq.68
  34.2 0.1 fusion.40
  34.3 0.1 reduce_window_sum.11
  34.4 0.2 select_reduce_fusion
  34.6 0.1 reduce_sum.64
  34.7 0.1 copy.93
  34.8 0.1 fusion.45
  34.8 0.1 copy.94
  34.9 0.2 convolution_convert_fusion
  35.2 14.2 %all_to_all.15 = bf16[8,16,768]{2,1,0:T(8,128)(2,1)S(1)} all-to-all(bf16[8,16,768]{2,1,0:T(8,128)(2,1)S(1)} %bitcast.164), channel_id=1, replica_groups=mesh['grp'=4,'ex'=8,'tp'=8] {'ex'}, dimensions={0} | all-to-all | bytes 393216 | tf_op jit(solution)/shard_map/all_to_all | solution.py:129
  49.4 3.4 stack.3
  52.8 6.5 %all-to-all-start.1 = ((bf16[32,1,8,1,16,768]{5,4,2,3,1,0:T(8,128)(2,1)}), bf16[32,1,8,1,16,768]{5,4,2,3,1,0:T(8,128)(2,1)}, u32[]{:S(2)}, u32[]{:S(2)}) async-start(bf16[32,1,8,1,16,768]{5,4,2,3,1,0:T(8,128)(2,1)} %stack.3), calls=%async_computation.1 | async-start | bytes 12582912 | tf_op jit(solution)/shard_map/all_to_all | solution.py:12
  59.3 0.0 reduce-scatter.2.cloned.1.call-start
  59.3 4.5 copy.120
  63.8 135.9 %all-to-all-done.1 = bf16[32,1,8,1,16,768]{5,4,2,3,1,0:T(8,128)(2,1)} async-done(((bf16[32,1,8,1,16,768]{5,4,2,3,1,0:T(8,128)(2,1)}), bf16[32,1,8,1,16,768]{5,4,2,3,1,0:T(8,128)(2,1)}, u32[]{:S(2)}, u32[]{:S(2)}) %all-to-all-start.1) | async-done | bytes 6291488 | tf_op jit(solution)/shard_map/all_to_all | solution.py:12
  199.7 4.7 %convolution_bitcast_fusion.1 = f32[4,8,16,256]{3,2,1,0:T(8,128)S(1)} fusion(bf16[4,8,8,16,768]{4,3,2,1,0:T(8,128)(2,1)} %bitcast.22, bf16[8,768,256,1,1]{2,1,4,0,3:T(8,128)(2,1)S(1)} %bitcast.159), kind=kOutput, calls=%fused_computation.8 | convolution fusion | flops 1610612736 | bytes 9961472 | tf_op jit(solution)/shard_map/gtajcd,jtdf->jgacf/dot_general | solution.py:135
  204.4 4.7 %fusion.19 = bf16[4,8,16,256,1]{3,2,4,1,0:T(8,128)(2,1)S(1)} fusion(bf16[4,8,8,16,768]{4,3,2,1,0:T(8,128)(2,1)} %bitcast.22, bf16[8,768,256,1,1]{2,1,4,0,3:T(8,128)(2,1)S(1)} %bitcast.168, f32[4,8,16,256]{3,2,1,0:T(8,128)S(1)} %convolution_bitcast_fusion.1), kind=kOutput, calls=%fused_computation.15 | convolution fusion | flops 1611399168 | bytes 10223616 | tf_op jit(solution)/shard_map/gtajcd,jtdf->jgacf/dot_general | solution.py:138
  209.1 1.9 convert_bitcast_fusion
  211.1 3.5 copy.98
  214.6 0.0 reduce-scatter.2.cloned.1.call-update
  214.7 0.7 copy.102
  215.3 0.1 iota_compare_fusion.1
  215.5 218.4 %reduce-scatter.2.cloned.1.call-done = bf16[1,8,1,16,768]{4,3,1,0,2:T(8,128)(2,1)} async-done(((bf16[32,8,1,16,768]{4,3,1,0,2:T(8,128)(2,1)}), bf16[1,8,1,16,768]{4,3,1,0,2:T(8,128)(2,1)}) %reduce-scatter.2.cloned.1.call-update) | async-done | bytes 196624 | tf_op jit(solution)/shard_map/reduce_scatter | solution.py:147
  433.8 9.4 %all-to-all-start.2 = ((bf16[8,1,16,768]{3,2,1,0:T(8,128)(2,1)}), bf16[8,1,16,768]{3,2,1,0:T(8,128)(2,1)S(1)}, u32[]{:S(2)}, u32[]{:S(2)}) async-start(bf16[8,1,16,768]{3,2,1,0:T(8,128)(2,1)} %bitcast.165), calls=%async_computation.3 | async-start | bytes 393216 | tf_op jit(solution)/shard_map/all_to_all | solution.py:150
  443.2 5.8 %all-to-all-done.2 = bf16[8,1,16,768]{3,2,1,0:T(8,128)(2,1)S(1)} async-done(((bf16[8,1,16,768]{3,2,1,0:T(8,128)(2,1)}), bf16[8,1,16,768]{3,2,1,0:T(8,128)(2,1)S(1)}, u32[]{:S(2)}, u32[]{:S(2)}) %all-to-all-start.2) | async-done | bytes 196640 | tf_op jit(solution)/shard_map/all_to_all | solution.py:150
  449.1 0.2 fusion.42
  449.2 0.1 fusion.35
  449.3 0.7 copy.103
  (26 shorter events, 0.2 us)
Async XLA Ops:
  7.2 192.5 %copy-start = (bf16[1,6144,256]{2,1,0:T(8,128)(2,1)S(1)}, bf16[1,6144,256]{2,1,0:T(8,128)(2,1)}, u32[]{:S(2)}) copy-start(bf16[1,6144,256]{2,1,0:T(8,128)(2,1)} %param.23) | copy-start | bytes 9437188
  7.2 7.4 %copy-start.8 = (bf16[16,2,128]{2,1,0:T(2,128)(2,1)S(1)}, bf16[16,2,128]{2,1,0:T(2,128)(2,1)}, u32[]{:S(2)}) copy-start(bf16[16,2,128]{2,1,0:T(2,128)(2,1)} %param.16) | copy-start | bytes 24580
  9.8 5.2 %copy-start.7 = (bf16[16,1,512,128]{3,2,1,0:T(8,128)(2,1)S(1)}, bf16[16,1,512,128]{3,2,1,0:T(8,128)(2,1)}, u32[]{:S(2)}) copy-start(bf16[16,1,512,128]{3,2,1,0:T(8,128)(2,1)} %param.18) | copy-start | bytes 6291460
  13.0 2.5 copy-start.5
  13.0 2.5 copy-start.2
  13.0 2.6 copy-start.3
  52.8 146.9 %all-to-all-start.1 = ((bf16[32,1,8,1,16,768]{5,4,2,3,1,0:T(8,128)(2,1)}), bf16[32,1,8,1,16,768]{5,4,2,3,1,0:T(8,128)(2,1)}, u32[]{:S(2)}, u32[]{:S(2)}) async-start(bf16[32,1,8,1,16,768]{5,4,2,3,1,0:T(8,128)(2,1)} %stack.3), calls=%async_computation.1 | async-start | bytes 12582912 | tf_op jit(solution)/shard_map/all_to_all | solution.py:12
  59.3 374.5 %reduce-scatter.2.cloned.1.call-start = ((), (), s32[]{:S(2)}) async-start(), calls=%async_computation.4 | async-start | bytes 6488064 | tf_op jit(solution)/shard_map/reduce_scatter | solution.py:147
  199.7 4.7 %copy-start.6 = (bf16[1,6144,256]{2,1,0:T(8,128)(2,1)S(1)}, bf16[1,6144,256]{2,1,0:T(8,128)(2,1)}, u32[]{:S(2)}) copy-start(bf16[1,6144,256]{2,1,0:T(8,128)(2,1)} %param.24) | copy-start | bytes 9437188
  204.4 4.7 %copy-start.1 = (bf16[32,8,8,768]{3,2,1,0:T(8,128)(2,1)S(1)}, bf16[32,8,8,768]{3,2,1,0:T(8,128)(2,1)}, u32[]{:S(2)}) copy-start(bf16[32,8,8,768]{3,2,1,0:T(8,128)(2,1)} %copy.120) | copy-start | bytes 9437188
  214.6 0.8 copy-start.4
  433.8 15.2 %all-to-all-start.2 = ((bf16[8,1,16,768]{3,2,1,0:T(8,128)(2,1)}), bf16[8,1,16,768]{3,2,1,0:T(8,128)(2,1)S(1)}, u32[]{:S(2)}, u32[]{:S(2)}) async-start(bf16[8,1,16,768]{3,2,1,0:T(8,128)(2,1)} %bitcast.165), calls=%async_computation.3 | async-start | bytes 393216 | tf_op jit(solution)/shard_map/all_to_all | solution.py:150
Sparse Core Ops, SparseCore 0:
  214.8 218.9 reduce-scatter.1
